TPU v7x, 256 devices: a whole 4x4x8 slice. The times are simulated.
256 devices in a mesh: row: 32 (over x, z_hi, y), col: 8 (over z_lo, core).
Axes of the slice: x: 4, y: 4, z: 8 (z_hi: 2, z_lo: 4; z = z_hi * 4 + z_lo), core: 2. Of those that a mesh axis runs over, the one named last changes fastest.
Arguments:
- tile_values: bfloat16 [32, 8, 256, 128, 128], P('row', 'col'), may hold values from -0.125 to 0.125
- tile_coords: int32 [32, 8, 2, 256], P('row', 'col'), may hold values from 0 to 63, as said below
- tile_counts: int32 [32, 8], P('row', 'col'), may hold values from 32 to 256, as said below
- features: bfloat16 [8, 32, 256, 256], P('col', 'row'), may hold values from -6 to 6
- weight_matrix: bfloat16 [256, 256], replicated, may hold values from -0.375 to 0.375
- out_grad: bfloat16 [32, 8, 256, 256], P('row', 'col'), may hold values from -6 to 6
Outputs:
- activated: bfloat16 [32, 8, 256, 256], P('row', 'col')
- feature_grad: float32 [8, 32, 256, 256], P('col', 'row')
- weight_grad: float32 [256, 256], replicated
Inputs may be any that keep to these rules, and one draw needn't show every extreme that they name: `tile_coords`: each device's 256 slots name distinct tile positions; the tile row is below 16. `tile_counts`: some device has all 256 slots live.
All inputs are finite; a program needn't handle non-finite values.
Results may differ from a plain program's by a relative error of at most 0.015.
Values may be sent and summed in bfloat16 or wider, within the bound.
No kernel may reach another device: no remote copies, remote signals or barrier semaphores. Data moves between devices by JAX's collectives and lax.ppermute only.
A program may use at most 128 MiB of HBM per device.

v0:
```python
import math
import jax
import jax.numpy as jnp
from jax import lax
from jax.sharding import PartitionSpec as P


def aggregate(values, pick_index, place_index, live_count, source, segments, transposed):
    slot_total = values.shape[0]
    block_size = math.gcd(slot_total, 32)
    tile_side = values.shape[1]
    width = source.shape[2]

    def block_step(block, totals):
        offset = block * block_size
        chosen = lax.dynamic_slice_in_dim(values, offset, block_size, 0)
        picks = lax.dynamic_slice_in_dim(pick_index, offset, block_size, 0)
        places = lax.dynamic_slice_in_dim(place_index, offset, block_size, 0)
        picked = source[picks]
        if transposed:
            products = jnp.einsum(
                "kij,kif->kjf", chosen, picked, preferred_element_type=jnp.float32
            )
        else:
            products = jnp.einsum(
                "kij,kjf->kif", chosen, picked, preferred_element_type=jnp.float32
            )
        is_live = offset + jnp.arange(block_size, dtype=jnp.int32) < live_count
        products = jnp.where(is_live[:, None, None], products, 0.0)
        return totals.at[places].add(products)

    start_totals = jnp.zeros((segments, tile_side, width), jnp.float32)
    upper = (live_count + block_size - 1) // block_size
    return lax.fori_loop(0, upper, block_step, start_totals)


def shards(tile_values, tile_coords, tile_counts, features, weight_matrix, out_grad):
    values = tile_values[0, 0]
    coords = tile_coords[0, 0]
    live_count = tile_counts[0, 0]
    tile_side = values.shape[1]
    sub_rows = features.shape[2]
    width = features.shape[3]
    n_col = lax.axis_size("col")
    row_tiles = n_col * sub_rows // tile_side
    column_block = lax.all_gather(features, "row", axis=1, tiled=True)
    col_source = column_block.reshape(-1, tile_side, width)
    col_tiles = col_source.shape[0]
    partial_value = aggregate(
        values, coords[1], coords[0], live_count, col_source, row_tiles, False
    )
    partial_value = partial_value.reshape(1, n_col, sub_rows, width)
    share = lax.psum_scatter(partial_value, "col", scatter_dimension=1, tiled=True)
    mixed = share.astype(jnp.bfloat16).reshape(sub_rows, width)
    pre = jnp.dot(mixed, weight_matrix, preferred_element_type=jnp.float32)
    sigma = jax.nn.sigmoid(pre)
    activated = (pre * sigma).astype(jnp.bfloat16)
    pre_grad = (
        out_grad.reshape(sub_rows, width).astype(jnp.float32) * sigma * (1.0 + pre * (1.0 - sigma))
    ).astype(jnp.bfloat16)
    weight_terms = jnp.dot(mixed.T, pre_grad, preferred_element_type=jnp.float32)
    own_grad = jnp.dot(pre_grad, weight_matrix.T, preferred_element_type=jnp.float32).astype(
        jnp.bfloat16
    )
    mixed_grad = lax.all_gather(own_grad.reshape(1, 1, sub_rows, width), "col", axis=1, tiled=True)
    row_source = mixed_grad.reshape(row_tiles, tile_side, width)
    back_partial = aggregate(values, coords[0], coords[1], live_count, row_source, col_tiles, True)
    back_partial = back_partial.reshape(1, -1, sub_rows, width)
    feature_grad = lax.psum_scatter(back_partial, "row", scatter_dimension=1, tiled=True)
    weight_grad = lax.psum(weight_terms, ("row", "col"))
    return (activated.reshape(1, 1, sub_rows, width), feature_grad, weight_grad)


def solution(mesh):
    return jax.shard_map(
        shards,
        mesh=mesh,
        in_specs=(
            P("row", "col", None, None, None),
            P("row", "col", None, None),
            P("row", "col"),
            P("col", "row", None, None),
            P(),
            P("row", "col", None, None),
        ),
        out_specs=(P("row", "col", None, None), P("col", "row", None, None), P()),
        check_vma=False,
    )
```

profile of v0, /device:TPU:32, one launch (start us, length us, event | category | flops | bytes accessed | tf_op | source)
XLA Modules:
  0.0 863.9 jit_solution(18019783541457873077)
XLA Ops:
  9.4 115.5 %all-gather.4.cloned.1.call-done = bf16[1,32,256,256]{3,2,0,1:T(8,128)(2,1)} async-done(((bf16[1,1,256,256]{3,2,0,1:T(8,128)(2,1)}), bf16[1,32,256,256]{3,2,0,1:T(8,128)(2,1)}) %all-gather.4.cloned.1.call-update) | async-done | bytes 4194320 | tf_op jit(solution)/shard_map/all_gather | solution.py:46
  125.1 32.2 %while.20 = (s32[]{:T(128)}, f32[16,128,256]{2,1,0:T(8,128)S(1)}, s32[]{:T(128)}, s32[256]{0:T(256)S(1)}, s32[]{:T(128)}, /*index=5*/bf16[256,128,128]{2,1,0:T(8...) while((s32[]{:T(128)}, f32[16,128,256]{2,1,0:T(8,128)S(1)}, ...), condition=%wide.region_2.3_spmd, body=%wide.region_0.2_spmd.sunk | while | flops 270533888 | bytes 24122484 | solution.py:34
  125.9 4.2 gather_fusion
  130.1 4.6 convolution_select_fusion.4
  134.7 6.5 scatter_fusion
  142.0 4.2 gather_fusion
  146.2 4.6 convolution_select_fusion.4
  150.8 6.5 scatter_fusion
  157.3 1.3 copy-done.1
  158.7 128.7 %reduce-scatter.3.cloned.1.call-done = f32[1,1,256,256]{3,2,1,0:T(8,128)} async-done(((f32[1,8,256,256]{3,2,1,0:T(8,128)}), f32[1,1,256,256]{3,2,1,0:T(8,128)}) %reduce-scatter.3.cloned.1.call-update) | async-done | bytes 262160 | tf_op jit(solution)/shard_map/reduce_scatter | solution.py:53
  287.5 1.9 fusion.5
  289.3 0.9 convolution_convert_fusion
  290.3 12.0 %copy.11 = bf16[1,1,256,128,128]{3,4,2,1,0:T(8,128)(2,1)} copy(bf16[1,1,256,128,128]{4,3,2,1,0:T(8,128)(2,1)} %bitcast.38) | data formatting | bytes 16777216 | tf_op args[0]
  302.3 0.9 fusion.6
  303.3 23.7 %all-gather.6.cloned.1.call-done = bf16[2048,256]{1,0:T(8,128)(2,1)} async-done(((bf16[256,256]{1,0:T(8,128)(2,1)}), bf16[2048,256]{1,0:T(8,128)(2,1)}) %all-gather.6.cloned.1.call-update) | async-done | bytes 1048592 | tf_op jit(solution)/shard_map/all_gather | solution.py:65
  327.0 4.3 broadcast_in_dim.41
  331.3 30.8 %while.21 = (s32[]{:T(128)}, f32[64,128,256]{2,1,0:T(8,128)}, s32[]{:T(128)}, s32[256]{0:T(256)S(1)}, s32[]{:T(128)}, /*index=5*/bf16[256,128,128]{1,2,0:T(8,128...) while((s32[]{:T(128)}, f32[64,128,256]{2,1,0:T(8,128)}, ...), condition=%wide.region_6.7_spmd, body=%wide.region_4.6_spmd.sunk | while | flops 270533888 | bytes 24122484 | solution.py:34
  332.7 3.9 convolution_select_fusion.5
  336.6 10.0 %scatter_fusion.1 = f32[64,128,256]{2,1,0:T(8,128)} fusion(f32[64,128,256]{2,1,0:T(8,128)} %get-tuple-element.304, s32[32]{0:T(128)S(1)} %get-tuple-element.253, f32[32,128,256]{2,1,0:T(8,128)} %convolution_select_fusion.5), kind=kCustom, calls=%fused_computation.3.clone.1 | custom fusion | flops 1048576 | bytes 12583040 | tf_op jit(solution)/shard_map/while/body/scatter-add | solution.py:30
  348.0 3.9 convolution_select_fusion.5
  351.9 10.2 %scatter_fusion.1 = f32[64,128,256]{2,1,0:T(8,128)} fusion(f32[64,128,256]{2,1,0:T(8,128)} %get-tuple-element.304, s32[32]{0:T(128)S(1)} %get-tuple-element.253, f32[32,128,256]{2,1,0:T(8,128)} %convolution_select_fusion.5), kind=kCustom, calls=%fused_computation.3.clone.1 | custom fusion | flops 1048576 | bytes 12583040 | tf_op jit(solution)/shard_map/while/body/scatter-add | solution.py:30
  362.1 224.9 %all-reduce.2.cloned.1.call-done = f32[256,256]{1,0:T(8,128)} async-done(((f32[256,256]{1,0:T(8,128)}), f32[256,256]{1,0:T(8,128)}) %all-reduce.2.cloned.1.call-update) | async-done | bytes 262160 | tf_op jit(solution)/shard_map/psum | solution.py:70
  586.9 268.8 %reduce-scatter.5.cloned.1.call-done = f32[1,1,256,256]{3,2,1,0:T(8,128)} async-done(((f32[1,32,256,256]{3,2,1,0:T(8,128)}), f32[1,1,256,256]{3,2,1,0:T(8,128)}) %reduce-scatter.5.cloned.1.call-update) | async-done | bytes 262160 | tf_op jit(solution)/shard_map/reduce_scatter | solution.py:69
  855.7 1.7 copy.31
  (35 shorter events, 6.3 us)
Async XLA Ops:
  7.2 280.3 %copy-start = (bf16[256,256]{1,0:T(8,128)(2,1)S(1)}, bf16[256,256]{1,0:T(8,128)(2,1)}, u32[]{:S(2)}) copy-start(bf16[256,256]{1,0:T(8,128)(2,1)} %param.14) | copy-start | bytes 393220
  7.2 117.7 %all-gather.4.cloned.1.call-start = ((), (), s32[]{:S(2)}) async-start(), calls=%async_computation.2 | async-start | bytes 4325376 | tf_op jit(solution)/shard_map/all_gather | solution.py:46
  7.9 279.5 %reduce-scatter.3.cloned.1.call-start = ((), (), s32[]{:S(2)}) async-start(), calls=%async_computation.3 | async-start | bytes 2359296 | tf_op jit(solution)/shard_map/reduce_scatter | solution.py:53
  125.1 162.4 %copy-start.4 = (bf16[1,1,256,256]{3,2,1,0:T(8,128)(2,1)S(1)}, bf16[1,1,256,256]{3,2,1,0:T(8,128)(2,1)}, u32[]{:S(2)}) copy-start(bf16[1,1,256,256]{3,2,1,0:T(8,128)(2,1)} %param.15) | copy-start | bytes 393220
  157.3 1.3 copy-start.1
  158.7 168.3 %all-gather.6.cloned.1.call-start = ((), (), s32[]{:S(2)}) async-start(), calls=%async_computation.6 | async-start | bytes 1179648 | tf_op jit(solution)/shard_map/all_gather | solution.py:65
  290.2 296.7 %all-reduce.2.cloned.1.call-start = ((), (), s32[]{:S(2)}) async-start(), calls=%async_computation.5 | async-start | bytes 524288 | tf_op jit(solution)/shard_map/psum | solution.py:70
  290.3 12.0 %copy-start.3 = (f32[1,1,256,256]{3,2,1,0:T(8,128)S(1)}, f32[1,1,256,256]{3,2,1,0:T(8,128)}, u32[]{:S(2)}) copy-start(f32[1,1,256,256]{3,2,1,0:T(8,128)} %reduce-scatter.3.cloned.1.call-done) | copy-start | bytes 786436
  303.3 552.5 %reduce-scatter.5.cloned.1.call-start = ((), (), s32[]{:S(2)}) async-start(), calls=%async_computation.4 | async-start | bytes 8650752 | tf_op jit(solution)/shard_map/reduce_scatter | solution.py:69
  327.0 4.3 copy-start.2
Sparse Core Ops, SparseCore 0:
  11.5 113.3 all-gather.3
  158.8 128.6 reduce-scatter.2
  290.4 36.5 all-gather.5
  332.9 254.0 all-reduce.1
  589.9 265.7 reduce-scatter.4
where the time goes:
time: 866 us; the launch traced here: 864 us
  waiting for transfers between devices  762 us (88%)
  other arithmetic  36.1 us (4%)
  local copies, waits for them, and re-layouts  30.1 us (3%)
  matrix products  20.6 us (2%)
  between operations  14.5 us (2%)
    reduce_scatter x1, waiting for transfers between devices, shards(): lax.psum_scatter(back_partial, 'row', scatter_dimension=1, tiled=True)  269 us
    psum x1, waiting for transfers between devices, shards(): weight_grad = lax.psum(weight_terms, ('row', 'col'))  225 us
    reduce_scatter x1, waiting for transfers between devices, shards(): lax.psum_scatter(partial_value, 'col', scatter_dimension=1, tiled=True)  129 us
    all_gather x1, waiting for transfers between devices, shards(): column_block = lax.all_gather(features, 'row', axis=1, tiled=True)  115 us
    scatter-add x4, other arithmetic, block_step(): return totals.at[places].add(products)  33.1 us
    all_gather x1, waiting for transfers between devices, shards(): lax.all_gather(own_grad.reshape(1, 1, sub_rows, width), 'col', axis=1, ti...  23.7 us
  transfers between devices with their start and end apart: 5, of which 5 were waited for; matrix products, arithmetic and copies ran while one was open for 6% of the time, Pallas kernels for 0%

commit v1 on v0

--- a/solution.py
+++ b/solution.py
@@ -67,7 +67,8 @@
     back_partial = aggregate(values, coords[0], coords[1], live_count, row_source, col_tiles, True)
     back_partial = back_partial.reshape(1, -1, sub_rows, width)
     feature_grad = lax.psum_scatter(back_partial, "row", scatter_dimension=1, tiled=True)
-    weight_grad = lax.psum(weight_terms, ("row", "col"))
+    terms = lax.all_gather(weight_terms, ("row", "col"))
+    weight_grad = jnp.sum(terms, axis=0)
     return (activated.reshape(1, 1, sub_rows, width), feature_grad, weight_grad)
 
 

time: 866 us -> 1090 us (1.26)
  waiting for transfers between devices: 762 us -> 956 us
  other arithmetic: 36.1 us -> 58.3 us
    all_gather x0 -> x1, waiting for transfers between devices: none -> 452 us  [shards(): terms = lax.all_gather(weight_terms, ('row', 'col'))]
    psum x1 -> x0, waiting for transfers between devices: 225 us -> none  [shards(): weight_grad = lax.psum(weight_terms, ('row', 'col'))]
    reduce_scatter x1, waiting for transfers between devices: 269 us -> 236 us  [shards(): lax.psum_scatter(back_partial, 'row', scatter_dimension=1, tiled=True)]
    reduce_sum x0 -> x1, other arithmetic: none -> 21.9 us  [shards(): weight_grad = jnp.sum(terms, axis=0)]
  transfers between devices with their start and end apart: 5 -> 5, of which waited for: 5 -> 5; matrix products, arithmetic and copies ran while one was open for 6% -> 7% of each run, Pallas kernels for 0% -> 0%
where the time goes in v1:
time: 1090 us; the launch traced here: 1080 us
  waiting for transfers between devices  956 us (88%)
  other arithmetic  58.3 us (5%)
  local copies, waits for them, and re-layouts  28.4 us (3%)
  matrix products  21.7 us (2%)
  between operations  14.5 us (1%)
    all_gather x1, waiting for transfers between devices, shards(): terms = lax.all_gather(weight_terms, ('row', 'col'))  452 us
    reduce_scatter x1, waiting for transfers between devices, shards(): lax.psum_scatter(back_partial, 'row', scatter_dimension=1, tiled=True)  236 us
    reduce_scatter x1, waiting for transfers between devices, shards(): lax.psum_scatter(partial_value, 'col', scatter_dimension=1, tiled=True)  129 us
    all_gather x1, waiting for transfers between devices, shards(): column_block = lax.all_gather(features, 'row', axis=1, tiled=True)  115 us
    scatter-add x4, other arithmetic, block_step(): return totals.at[places].add(products)  33.5 us
    all_gather x1, waiting for transfers between devices, shards(): lax.all_gather(own_grad.reshape(1, 1, sub_rows, width), 'col', axis=1, ti...  22.7 us
    reduce_sum x1, other arithmetic, shards(): weight_grad = jnp.sum(terms, axis=0)  21.9 us
  transfers between devices with their start and end apart: 5, of which 5 were waited for; matrix products, arithmetic and copies ran while one was open for 7% of the time, Pallas kernels for 0%

profile of v1, /device:TPU:32, one launch (start us, length us, event | category | flops | bytes accessed | tf_op | source)
XLA Modules:
  0.0 1078.8 jit_solution(14926338428255874310)
XLA Ops:
  9.4 115.5 %all-gather.6.cloned.1.call-done = bf16[1,32,256,256]{3,2,0,1:T(8,128)(2,1)} async-done(((bf16[1,1,256,256]{3,2,0,1:T(8,128)(2,1)}), bf16[1,32,256,256]{3,2,0,1:T(8,128)(2,1)}) %all-gather.6.cloned.1.call-update) | async-done | bytes 4194320 | tf_op jit(solution)/shard_map/all_gather | solution.py:46
  125.1 32.2 %while.20 = (s32[]{:T(128)}, f32[16,128,256]{2,1,0:T(8,128)S(1)}, s32[]{:T(128)}, s32[256]{0:T(256)S(1)}, s32[]{:T(128)}, /*index=5*/bf16[256,128,128]{2,1,0:T(8...) while((s32[]{:T(128)}, f32[16,128,256]{2,1,0:T(8,128)S(1)}, ...), condition=%wide.region_2.3_spmd, body=%wide.region_0.2_spmd.sunk | while | flops 270533888 | bytes 24122492 | solution.py:34
  125.2 4.2 gather_fusion
  130.1 4.6 convolution_select_fusion.4
  134.7 6.5 scatter_fusion
  141.3 4.2 gather_fusion
  146.2 4.6 convolution_select_fusion.4
  150.8 6.5 scatter_fusion
  157.3 1.3 copy-done.1
  158.7 128.9 %reduce-scatter.3.cloned.1.call-done = f32[1,1,256,256]{3,2,1,0:T(8,128)} async-done(((f32[1,8,256,256]{3,2,1,0:T(8,128)}), f32[1,1,256,256]{3,2,1,0:T(8,128)}) %reduce-scatter.3.cloned.1.call-update) | async-done | bytes 262160 | tf_op jit(solution)/shard_map/reduce_scatter | solution.py:53
  287.6 1.9 fusion.5
  289.5 0.9 convolution_convert_fusion
  290.4 1.9 fusion.6
  292.4 12.0 %copy.11 = bf16[1,1,256,128,128]{3,4,2,1,0:T(8,128)(2,1)} copy(bf16[1,1,256,128,128]{4,3,2,1,0:T(8,128)(2,1)} %bitcast.39) | data formatting | bytes 16777216 | tf_op args[0]
  304.4 22.7 %all-gather.8.cloned.1.call-done = bf16[2048,256]{1,0:T(8,128)(2,1)} async-done(((bf16[256,256]{1,0:T(8,128)(2,1)}), bf16[2048,256]{1,0:T(8,128)(2,1)}) %all-gather.8.cloned.1.call-update) | async-done | bytes 1048592 | tf_op jit(solution)/shard_map/all_gather | solution.py:65
  327.1 4.4 broadcast_in_dim.41
  331.4 31.2 %while.21 = (s32[]{:T(128)}, f32[64,128,256]{2,1,0:T(8,128)}, s32[]{:T(128)}, s32[256]{0:T(256)S(1)}, s32[]{:T(128)}, /*index=5*/bf16[256,128,128]{1,2,0:T(8,128...) while((s32[]{:T(128)}, f32[64,128,256]{2,1,0:T(8,128)}, ...), condition=%wide.region_6.7_spmd, body=%wide.region_4.6_spmd.sunk | while | flops 270533888 | bytes 24122492 | solution.py:34
  332.8 3.9 convolution_select_fusion.5
  336.8 10.2 scatter_fusion.1
  348.4 4.0 convolution_select_fusion.5
  352.4 10.3 scatter_fusion.1
  362.6 451.9 %all-gather.10.cloned.1.call-done = f32[65536,256]{1,0:T(8,128)} async-done(((f32[256,256]{1,0:T(8,128)}), f32[65536,256]{1,0:T(8,128)}) %all-gather.10.cloned.1.call-update) | async-done | bytes 67108880 | tf_op jit(solution)/shard_map/all_gather | solution.py:70
  814.6 21.9 %reduce_sum.9 = f32[256,256]{1,0:T(8,128)} reduce(f32[256,256,256]{2,1,0:T(8,128)} %bitcast.13, f32[]{:T(128)} %constant.52.clone.1), dimensions={0}, to_apply=%region_8.9 | reduce | flops 16711680 | bytes 67371008 | tf_op jit(solution)/shard_map/reduce_sum | solution.py:71
  836.5 235.8 %reduce-scatter.5.cloned.1.call-done = f32[1,1,256,256]{3,2,1,0:T(8,128)} async-done(((f32[1,32,256,256]{3,2,1,0:T(8,128)}), f32[1,1,256,256]{3,2,1,0:T(8,128)}) %reduce-scatter.5.cloned.1.call-update) | async-done | bytes 262160 | tf_op jit(solution)/shard_map/reduce_scatter | solution.py:69
  (33 shorter events, 6.2 us)
Async XLA Ops:
  7.2 280.4 %copy-start = (bf16[256,256]{1,0:T(8,128)(2,1)S(1)}, bf16[256,256]{1,0:T(8,128)(2,1)}, u32[]{:S(2)}) copy-start(bf16[256,256]{1,0:T(8,128)(2,1)} %param.14) | copy-start | bytes 393220
  7.2 117.7 %all-gather.6.cloned.1.call-start = ((), (), s32[]{:S(2)}) async-start(), calls=%async_computation.2 | async-start | bytes 4325376 | tf_op jit(solution)/shard_map/all_gather | solution.py:46
  7.9 279.7 %reduce-scatter.3.cloned.1.call-start = ((), (), s32[]{:S(2)}) async-start(), calls=%async_computation.3 | async-start | bytes 2359296 | tf_op jit(solution)/shard_map/reduce_scatter | solution.py:53
  125.1 162.5 %copy-start.3 = (bf16[1,1,256,256]{3,2,1,0:T(8,128)(2,1)S(1)}, bf16[1,1,256,256]{3,2,1,0:T(8,128)(2,1)}, u32[]{:S(2)}) copy-start(bf16[1,1,256,256]{3,2,1,0:T(8,128)(2,1)} %param.15) | copy-start | bytes 393220
  157.3 1.3 copy-start.1
  158.6 168.4 %all-gather.8.cloned.1.call-start = ((), (), s32[]{:S(2)}) async-start(), calls=%async_computation.5 | async-start | bytes 1179648 | tf_op jit(solution)/shard_map/all_gather | solution.py:65
  290.4 524.2 %all-gather.10.cloned.1.call-start = ((), (), s32[]{:S(2)}) async-start(), calls=%async_computation.6 | async-start | bytes 67371008 | tf_op jit(solution)/shard_map/all_gather | solution.py:70
  292.3 780.0 %reduce-scatter.5.cloned.1.call-start = ((), (), s32[]{:S(2)}) async-start(), calls=%async_computation.4 | async-start | bytes 8650752 | tf_op jit(solution)/shard_map/reduce_scatter | solution.py:69
  327.1 4.4 copy-start.2
Sparse Core Ops, SparseCore 0:
  11.5 113.3 all-gather.5
  158.7 128.8 reduce-scatter.2
  290.5 36.5 all-gather.7
  329.4 485.1 all-gather.9
  817.5 254.7 reduce-scatter.4
